TPU v7x, 256 devices: a whole 4x4x8 slice. The times are simulated.
256 devices in a mesh: dp: 64 (over y, z_lo, x), tensor: 4 (over z_hi, core).
Axes of the slice: x: 4, y: 4, z: 8 (z_hi: 2, z_lo: 4; z = z_hi * 4 + z_lo), core: 2. Of those that a mesh axis runs over, the one named last changes fastest.
Arguments:
- tokens: bfloat16 [16384, 8192], P('dp', 'tensor'), may hold values from -160 to 160
- weights: bfloat16 [3, 512, 32, 256], P(None, None, 'tensor'), may hold values from -0.25 to 0.25
- cotangent: bfloat16 [16384, 8192], P('dp', 'tensor'), may hold values from -6 to 6
Outputs:
- mixed: bfloat16 [16384, 8192], P('dp', 'tensor')
- token_grads: bfloat16 [16384, 8192], P('dp', 'tensor')
- weight_grads: float32 [3, 512, 32, 256], P(None, 'dp', 'tensor')
All inputs are finite; a program needn't handle non-finite values.
Results may differ from a plain program's by a relative error of at most 0.0014.
The roundings to bfloat16 on the way count: a program that leaves them out, or rounds other values in their place, can miss the bound.
Values may be sent and summed in bfloat16 or wider, within the bound.
No kernel may reach another device: no remote copies, remote signals or barrier semaphores. Data moves between devices by JAX's collectives and lax.ppermute only.
A program may use at most 128 MiB of HBM per device.

v0:
```python
import math
import jax
import jax.numpy as jnp
from jax import lax
from jax.sharding import Mesh, PartitionSpec as P

D = 8192
BLK = 256
FACTORS = 3
root_half = 0.7071067811865476
pdf_scale = 0.3989422804014327
epsilon = 1e-06


def swapped(x, axis, stride):
    return lax.ppermute(x, axis, [(i, i ^ 1 << stride) for i in range(lax.axis_size(axis))])


def tensor_sum(x):
    for bit in range(lax.axis_size("tensor").bit_length() - 1):
        x = x + swapped(x, "tensor", bit)
    return x


def scatter_first(grads):
    rows = grads.shape[0]
    ny, nz, nx = (lax.axis_size(a) for a in ("dy", "dz", "dx"))
    rest = grads.shape[1:]
    share = rows // (ny * nz * nx)
    g = lax.psum_scatter(grads.reshape(ny, -1, rest[-1]), "dy", scatter_dimension=0, tiled=True)
    return g.reshape((nz, nx, share) + rest)


def exchange_first(grads):
    rows = grads.shape[0]
    ny, nz, nx = (lax.axis_size(a) for a in ("dy", "dz", "dx"))
    rest = grads.shape[1:]
    g = grads.reshape((ny, nz, nx, rows // (ny * nz * nx)) + rest)
    return jnp.sum(lax.all_to_all(g, "dx", 2, 2), axis=2)


def scatter_rest(on_sc, on_tc):
    nz, nx, share = on_sc[0].shape[:3]
    rest = on_sc[0].shape[3:]
    a, on_tc = lax.optimization_barrier((jnp.stack(on_sc, axis=0), on_tc))
    a = jnp.moveaxis(a, 2, 0)
    a = lax.psum_scatter(a.reshape(nx, -1, rest[-1]), "dx", scatter_dimension=0, tiled=True)
    a = a.reshape((len(on_sc), nz, share) + rest)
    b = jnp.sum(lax.all_to_all(on_tc, "dy", 0, 0), axis=0)
    g = jnp.moveaxis(jnp.concatenate([b[None], a], axis=0), 1, 0)
    return jnp.sum(lax.all_to_all(g, "dz", 0, 0), axis=0)


def partner_rows(rows):
    pieces = lax.axis_size(("dy", "dx"))
    piece = rows.shape[0] // pieces
    mine = lax.axis_index("dy") * lax.axis_size("dx") + lax.axis_index("dx")
    part = lax.dynamic_slice_in_dim(rows, mine * piece, piece, axis=0)
    part = swapped(part, "tensor", 1)
    return lax.all_gather(part, ("dy", "dx"), axis=0, tiled=True)


def gelu_value(value):
    return value * (0.5 * (1.0 + lax.erf(value * root_half)))


def gelu_slope(value):
    return (
        0.5 * (1.0 + lax.erf(value * root_half)) + value * jnp.exp(-0.5 * value * value) * pdf_scale
    )


def local_partner(blocks, stride):
    tok_rows, block_count, width = blocks.shape
    folded = blocks.reshape(tok_rows, block_count // (2 * stride), 2, stride, width)
    return jnp.flip(folded, axis=2).reshape(tok_rows, block_count, width)


def apply_factor(hidden, partner, layer_weights):
    preact = jnp.einsum(
        "tbc,cbd->tbd", hidden, layer_weights[:BLK], preferred_element_type=jnp.float32
    )
    return preact + jnp.einsum(
        "tbc,cbd->tbd", partner, layer_weights[BLK:], preferred_element_type=jnp.float32
    )


def shards(tokens, weights, cotangent):
    tok_rows, local_width = tokens.shape
    blocks_dev = local_width // BLK
    block_bits = (D // BLK).bit_length() - 1
    device_bits = blocks_dev.bit_length() - 1
    data_size = lax.axis_size(("dy", "dz", "dx"))
    grad_scale = 1.0 / math.sqrt(tok_rows * data_size)
    top = FACTORS - 1
    assert block_bits - 1 - device_bits == 1
    cot_blocks = cotangent.reshape(tok_rows, blocks_dev, BLK)
    partner_cot = swapped(cot_blocks, "tensor", 1)
    tokens_f32 = tokens.astype(jnp.float32)
    square_sum = tensor_sum(jnp.sum(tokens_f32 * tokens_f32, axis=1))
    inv_rms = lax.rsqrt(square_sum / D + epsilon)[:, None]
    normed = tokens_f32 * inv_rms
    hidden = normed.astype(jnp.bfloat16).reshape(tok_rows, blocks_dev, BLK)
    stored_inputs = []
    stored_preact = []
    for factor in range(top):
        bit_index = block_bits - FACTORS + factor
        stride = 1 << bit_index
        if stride < blocks_dev:
            partner = local_partner(hidden, stride)
        else:
            partner = swapped(hidden, "tensor", bit_index - device_bits)
        preact = apply_factor(hidden, partner, weights[factor])
        stored_inputs.append((hidden, partner))
        stored_preact.append(preact)
        hidden = gelu_value(preact).astype(jnp.bfloat16)
    hidden, partner_cot = lax.optimization_barrier((hidden, partner_cot))
    partner_top = swapped(hidden, "tensor", 1)
    top_weights = weights[top]
    grad_hidden = jnp.einsum(
        "tbd,cbd->tbc", cot_blocks, top_weights[:BLK], preferred_element_type=jnp.float32
    ) + jnp.einsum(
        "tbd,cbd->tbc",
        partner_cot,
        partner_rows(top_weights[BLK:]),
        preferred_element_type=jnp.float32,
    )
    grad_pre = (grad_hidden * gelu_slope(stored_preact[top - 1])).astype(jnp.bfloat16)
    grad_terms = [None] * FACTORS
    for factor in reversed(range(top)):
        bit_index = block_bits - FACTORS + factor
        stride = 1 << bit_index
        kept_hidden, kept_partner = stored_inputs[factor]
        joined = jnp.concatenate([kept_hidden, kept_partner], axis=2)
        grad_terms[factor] = (exchange_first if factor == 0 else scatter_first)(
            jnp.einsum("tbc,tbd->cbd", joined, grad_pre, preferred_element_type=jnp.float32)
            * grad_scale
        )
        layer_weights = weights[factor]
        near_term = jnp.einsum(
            "tbd,cbd->tbc", grad_pre, layer_weights[:BLK], preferred_element_type=jnp.float32
        )
        far_term = jnp.einsum(
            "tbd,cbd->tbc", grad_pre, layer_weights[BLK:], preferred_element_type=jnp.float32
        )
        if stride < blocks_dev:
            arrived = local_partner(far_term, stride)
        else:
            arrived = swapped(far_term, "tensor", bit_index - device_bits)
        grad_hidden = near_term + arrived
        if factor > 0:
            previous = stored_preact[factor - 1]
            grad_pre = (grad_hidden * gelu_slope(previous)).astype(jnp.bfloat16)
    partner_top, _ = lax.optimization_barrier((partner_top, grad_hidden))
    preact = apply_factor(hidden, partner_top, top_weights)
    mixed = (tokens_f32 + preact.reshape(tok_rows, local_width)).astype(jnp.bfloat16)
    joined = jnp.concatenate([hidden, partner_top], axis=2)
    grad_terms[top] = scatter_first(
        jnp.einsum("tbc,tbd->cbd", joined, cot_blocks, preferred_element_type=jnp.float32)
        * grad_scale
    )
    flat = grad_hidden.reshape(tok_rows, local_width)
    inner_sum = tensor_sum(jnp.sum(flat * normed, axis=1))
    token_grads = (
        cotangent.astype(jnp.float32) + inv_rms * (flat - normed * (inner_sum / D)[:, None])
    ).astype(jnp.bfloat16)
    weight_grads = scatter_rest(grad_terms[1:], grad_terms[0])
    return (mixed, token_grads, weight_grads)


def solution(mesh):
    ny, nz, nx = (4, 4, 4)
    fine = Mesh(
        mesh.devices.reshape(ny, nz, nx, mesh.shape["tensor"]), ("dy", "dz", "dx", "tensor")
    )
    dp = ("dy", "dz", "dx")
    return jax.shard_map(
        shards,
        mesh=fine,
        in_specs=(P(dp, "tensor"), P(None, None, "tensor", None), P(dp, "tensor")),
        out_specs=(P(dp, "tensor"), P(dp, "tensor"), P(None, dp, "tensor", None)),
        check_vma=False,
    )
```

profile of v0, /device:TPU:1, one launch (start us, length us, event | category | flops | bytes accessed | tf_op | source)
XLA Modules:
  0.0 300.6 jit_solution(10783310645281897651)
XLA Ops:
  7.2 1.5 copy.117
  9.0 3.3 %collective-permute-start = (f32[256]{0:T(256)S(1)}, f32[256]{0:T(256)S(1)}, u32[]{:S(2)}, u32[]{:S(2)}) collective-permute-start(f32[256]{0:T(256)S(1)} %fusion.8), channel_id=1, source_target_pairs={{0,1},{1,0},{2,3},{3,2},{4,5},{5,4},{6,7},{7,6},{8,9},{9,8},{10,11... | collective-permute-start | bytes 3080 | tf_op jit(solution)/shard_map/ppermute | solution.py:16
  12.3 5.2 %fusion.54 = (bf16[1,256,8,256]{3,2,1,0:T(8,128)(2,1)}, bf16[1,256,8,256]{3,2,1,0:T(8,128)(2,1)}, bf16[1,256,8,256]{3,2,1,0:T(8,128)(2,1)}, bf16[1,256,8,256]{3,...) fusion(bf16[3,512,8,256]{3,2,1,0:T(8,128)(2,1)} %param.4), kind=kLoop, calls=%fused_computation.80 | loop fusion | bytes 12582912 | tf_op jit(solution)/shard_map/slice | solution.py:84
  17.5 1.6 copy.182
  19.2 5.3 %collective-permute-start.1 = (f32[256]{0:T(256)S(1)}, f32[256]{0:T(256)S(1)}, u32[]{:S(2)}, u32[]{:S(2)}) collective-permute-start(f32[256]{0:T(256)S(1)} %add.80), channel_id=1, source_target_pairs={{0,2},{1,3},{2,0},{3,1},{4,6},{5,7},{6,4},{7,5},{8,10},{9,11},{10,... | collective-permute-start | bytes 3080 | tf_op jit(solution)/shard_map/ppermute | solution.py:16
  24.5 1.0 constant_dynamic-slice_fusion
  25.5 1.2 copy.134
  27.0 2.4 copy.179
  29.4 1.6 copy.178
  31.3 1.3 copy.120
  32.6 1.3 rev.8
  33.9 0.7 copy-done.18
  34.7 1.8 fusion.46
  36.5 2.3 fusion.38
  38.8 1.3 collective-permute-start.2
  40.2 1.0 copy.197
  41.2 4.4 %collective-permute-start.3 = (bf16[256,8,256]{2,0,1:T(8,128)(2,1)}, bf16[256,8,256]{2,0,1:T(8,128)(2,1)}, u32[]{:S(2)}, u32[]{:S(2)}) collective-permute-start(bf16[256,8,256]{2,0,1:T(8,128)(2,1)} %bitcast.127), channel_id=1, source_target_pairs={{0,2},{1,3},{2,0},{3,1},{4,6},{5,7},{6,4},{7,5},{8,10},{9,11},{10,... | collective-permute-start | bytes 3145736 | tf_op jit(solution)/shard_map/ppermute | solution.py:16
  45.6 1.6 copy.177
  47.3 1.8 fusion.41
  49.3 1.8 fusion.50
  51.1 3.7 %fusion.34 = (bf16[256,8,256]{0,2,1:T(8,128)(2,1)}, f32[8,256,256]{1,2,0:T(8,128)}) fusion(f32[8,256,256]{1,2,0:T(8,128)S(1)} %fusion.50, bf16[256,8,256]{0,2,1:T(8,128)(2,1)} %collective-permute-done.2, bf16[1,256,8,256]{3,2,1,0:T(8,128)(2,1)S(1)} %copy-done.3), kind=kOutput, calls=%fused_computation.47 | convolution fusion | flops 271581184 | bytes 7340032 | tf_op jit(solution)/shard_map/tbc,cbd->tbd/dot_general | solution.py:83
  54.8 21.4 %collective-permute-done.3 = bf16[256,8,256]{2,0,1:T(8,128)(2,1)} collective-permute-done((bf16[256,8,256]{2,0,1:T(8,128)(2,1)}, bf16[256,8,256]{2,0,1:T(8,128)(2,1)}, u32[]{:S(2)}, u32[]{:S(2)}) %collective-permute-start.3) | collective-permute-done | bytes 1048608 | tf_op jit(solution)/shard_map/ppermute | solution.py:16
  76.2 6.7 %all-gather.2.cloned.1.call-done = bf16[256,8,256]{2,0,1:T(8,128)(2,1)} async-done(((bf16[16,8,256]{2,0,1:T(8,128)(2,1)}), bf16[256,8,256]{2,0,1:T(8,128)(2,1)}) %all-gather.2.cloned.1.call-update) | async-done | bytes 1048592 | tf_op jit(solution)/shard_map/all_gather | solution.py:60
  82.9 4.0 %fusion.15 = bf16[256,8,256]{0,2,1:T(8,128)(2,1)S(1)} fusion(f32[8,256,256]{1,2,0:T(8,128)} %get-tuple-element.33, f32[8,256,256]{2,1,0:T(8,128)} %fusion.41, bf16[256,8,256]{2,0,1:T(8,128)(2,1)} %all-gather.2.cloned.1.call-done, bf16[256,8,256]{2,0,1:T(8,128)(2,1)} %collective-permute-done.3), kind=kOutput, calls=%fused_computation.23 | convolution fusion | flops 274202624 | bytes 7340032 | tf_op jit(solution)/shard_map/tbd,cbd->tbc/dot_general | solution.py:122
  86.9 1.0 copy-done.15
  87.8 4.3 %multiply_bitcast_fusion.2 = f32[512,8,256]{0,2,1:T(8,128)} fusion(bf16[256,8,256]{0,2,1:T(8,128)(2,1)S(1)} %fusion.15, bf16[256,8,256]{0,2,1:T(8,128)(2,1)} %collective-permute-done.2, bf16[256,8,256]{0,2,1:T(8,128)(2,1)} %get-tuple-element.30), kind=kOutput, calls=%fused_computation.2 | convolution fusion | flops 542113792 | bytes 7340032 | tf_op jit(solution)/shard_map/tbc,tbd->cbd/dot_general | solution.py:136
  92.1 5.4 %copy.147 = f32[512,8,256]{2,1,0:T(8,128)} copy(f32[512,8,256]{0,2,1:T(8,128)} %multiply_bitcast_fusion.2) | data formatting | bytes 8388608 | tf_op jit(solution)/shard_map/mul | solution.py:136
  97.7 1.8 convolution_bitcast_fusion
  99.5 2.3 collective-permute-start.6
  101.8 5.5 %collective-permute-start.4 = (bf16[256,8,256]{0,2,1:T(8,128)(2,1)}, bf16[256,8,256]{0,2,1:T(8,128)(2,1)}, u32[]{:S(2)}, u32[]{:S(2)}) collective-permute-start(bf16[256,8,256]{0,2,1:T(8,128)(2,1)} %get-tuple-element.8), channel_id=1, source_target_pairs={{0,2},{1,3},{2,0},{3,1},{4,6},{5,7},{6,4},{7,5},{8,10},{9,11},{10,... | collective-permute-start | bytes 3145736 | tf_op jit(solution)/shard_map/ppermute | solution.py:16
  107.3 1.4 fusion.21
  108.7 0.5 fusion.44
  109.2 0.5 copy-done.6
  109.7 1.9 copy.143
  111.5 3.1 %rev.9 = f32[256,1,2,4,256]{0,4,3,2,1:T(8,128)} reverse(f32[256,1,2,4,256]{0,4,3,2,1:T(8,128)} %copy.143), dimensions={2} | reverse | bytes 4194304 | tf_op jit(solution)/shard_map/jit(_flip)/rev | solution.py:76
  114.6 2.8 bitcast_add_fusion
  117.4 13.7 %collective-permute-done.4 = bf16[256,8,256]{0,2,1:T(8,128)(2,1)} collective-permute-done((bf16[256,8,256]{0,2,1:T(8,128)(2,1)}, bf16[256,8,256]{0,2,1:T(8,128)(2,1)}, u32[]{:S(2)}, u32[]{:S(2)}) %collective-permute-start.4) | collective-permute-done | bytes 1048608 | tf_op jit(solution)/shard_map/ppermute | solution.py:16
  131.1 2.3 multiply_bitcast_fusion.1
  133.4 4.4 %copy.149 = f32[512,8,256]{2,1,0:T(8,128)} copy(f32[512,8,256]{2,0,1:T(8,128)S(1)} %multiply_bitcast_fusion.1) | data formatting | bytes 8388608 | tf_op jit(solution)/shard_map/mul | solution.py:159
  137.9 2.3 copy.152
  140.2 4.6 %multiply_bitcast_fusion = f32[512,8,256]{0,2,1:T(8,128)} fusion(bf16[256,8,256]{0,2,1:T(8,128)(2,1)} %copy-done.6, bf16[256,8,256]{2,0,1:T(8,128)(2,1)} %bitcast.138, bf16[256,8,256]{2,0,1:T(8,128)(2,1)} %copy.152), kind=kOutput, calls=%fused_computation | convolution fusion | flops 542113792 | bytes 7340032 | tf_op jit(solution)/shard_map/tbc,tbd->cbd/dot_general | solution.py:136
  144.7 5.4 %copy.153 = f32[512,8,256]{2,1,0:T(8,128)} copy(f32[512,8,256]{0,2,1:T(8,128)} %multiply_bitcast_fusion) | data formatting | bytes 8388608 | tf_op jit(solution)/shard_map/mul | solution.py:136
  150.2 2.6 copy.154
  152.8 30.1 %all_to_all.15 = f32[4,4,4,8,8,256]{5,4,3,1,0,2:T(8,128)} all-to-all(f32[4,4,4,8,8,256]{5,4,3,1,0,2:T(8,128)S(1)} %copy.154), channel_id=1, replica_groups=mesh['dy'=4,'dz'=4,'dx'=4,'tensor'=4] {'dx'}, dimensions={2} | all-to-all | bytes 8388608 | tf_op jit(solution)/shard_map/all_to_all | solution.py:39
  182.8 3.7 %reduce_sum.47 = f32[4,4,8,8,256]{4,3,2,1,0:T(8,128)} reduce(f32[4,4,4,8,8,256]{5,4,3,1,0,2:T(8,128)} %all_to_all.15, f32[]{:T(128)} %constant.7.clone.1), dimensions={2}, to_apply=%region_4.5 | reduce | flops 786432 | bytes 5242884 | tf_op jit(solution)/shard_map/reduce_sum | solution.py:39
  186.5 22.7 %reduce-scatter.6.cloned.1.call-done = f32[1,1024,256]{2,1,0:T(8,128)} async-done(((f32[4,1024,256]{2,1,0:T(8,128)}), f32[1,1024,256]{2,1,0:T(8,128)}) %reduce-scatter.6.cloned.1.call-update) | async-done | bytes 1048592 | tf_op jit(solution)/shard_map/reduce_scatter | solution.py:30
  209.2 1.7 pad_maximum_fusion
  210.9 1.5 copy.176
  212.4 4.3 %all-to-all-start.1 = ((f32[4,4,8,8,256]{4,3,2,1,0:T(8,128)}), f32[4,4,8,8,256]{4,3,2,1,0:T(8,128)}, u32[]{:S(2)}, u32[]{:S(2)}) async-start(f32[4,4,8,8,256]{4,3,2,1,0:T(8,128)} %reduce_sum.47), calls=%async_computation.3 | async-start | bytes 2097152 | tf_op jit(solution)/shard_map/all_to_all | solution.py:49
  216.7 2.3 copy.145
  219.3 0.9 collective-permute-start.7
  220.2 3.0 %fusion.39 = f32[8,256,256]{1,2,0:T(8,128)} fusion(bf16[256,8,256]{0,2,1:T(8,128)(2,1)} %collective-permute-done.4, bf16[1,256,8,256]{1,3,2,0:T(8,128)(2,1)S(1)} %copy-done.10), kind=kOutput, calls=%fused_computation.61 | convolution fusion | flops 268435456 | bytes 4194304 | tf_op jit(solution)/shard_map/tbc,cbd->tbd/dot_general | solution.py:83
  223.2 5.9 %collective-permute-start.8 = (f32[256]{0:T(256)S(1)}, f32[256]{0:T(256)S(1)}, u32[]{:S(2)}, u32[]{:S(2)}) collective-permute-start(f32[256]{0:T(256)S(1)} %add.101), channel_id=1, source_target_pairs={{0,2},{1,3},{2,0},{3,1},{4,6},{5,7},{6,4},{7,5},{8,10},{9,11},{10,... | collective-permute-start | bytes 3080 | tf_op jit(solution)/shard_map/ppermute | solution.py:16
  229.2 1.8 all-to-all-done.1
  231.0 1.3 reduce_sum.48
  232.4 33.5 %reduce-scatter.8.cloned.1.call-done = f32[1,512,256]{2,1,0:T(8,128)} async-done(((f32[4,512,256]{2,1,0:T(8,128)}), f32[1,512,256]{2,1,0:T(8,128)}) %reduce-scatter.8.cloned.1.call-update) | async-done | bytes 524304 | tf_op jit(solution)/shard_map/reduce_scatter | solution.py:47
  265.9 2.0 maximum_bitcast_fusion
  267.9 4.5 %all-to-all-start.2 = ((f32[4,3,8,8,256]{4,3,2,1,0:T(8,128)}), f32[4,3,8,8,256]{4,3,2,1,0:T(8,128)}, u32[]{:S(2)}, u32[]{:S(2)}) async-start(f32[4,3,8,8,256]{4,3,2,1,0:T(8,128)} %maximum_bitcast_fusion), calls=%async_computation.5 | async-start | bytes 1572864 | tf_op jit(solution)/shard_map/all_to_all | solution.py:51
  272.4 2.8 convolution_add_fusion
  275.2 1.9 fusion.7
  277.1 2.4 copy.157
  279.5 1.4 copy.158
  280.9 11.2 %all-to-all-done.2 = f32[4,3,8,8,256]{4,3,2,1,0:T(8,128)} async-done(((f32[4,3,8,8,256]{4,3,2,1,0:T(8,128)}), f32[4,3,8,8,256]{4,3,2,1,0:T(8,128)}, u32[]{:S(2)}, u32[]{:S(2)}) %all-to-all-start.2) | async-done | bytes 786464 | tf_op jit(solution)/shard_map/all_to_all | solution.py:51
  292.1 1.9 reduce_sum.49
  (59 shorter events, 1.7 us)
Async XLA Ops:
  7.2 75.7 %all-gather.2.cloned.1.call-start = ((), (), s32[]{:S(2)}) async-start(), calls=%async_computation.6 | async-start | bytes 1114112 | tf_op jit(solution)/shard_map/all_gather | solution.py:60
  9.0 10.2 %collective-permute-start = (f32[256]{0:T(256)S(1)}, f32[256]{0:T(256)S(1)}, u32[]{:S(2)}, u32[]{:S(2)}) collective-permute-start(f32[256]{0:T(256)S(1)} %fusion.8), channel_id=1, source_target_pairs={{0,1},{1,0},{2,3},{3,2},{4,5},{5,4},{6,7},{7,6},{8,9},{9,8},{10,11... | collective-permute-start | bytes 3080 | tf_op jit(solution)/shard_map/ppermute | solution.py:16
  19.2 11.9 %copy-start.9 = (bf16[1,256,8,256]{1,3,2,0:T(8,128)(2,1)}, bf16[1,256,8,256]{1,3,2,0:T(8,128)(2,1)S(1)}, u32[]{:S(2)}) copy-start(bf16[1,256,8,256]{1,3,2,0:T(8,128)(2,1)S(1)} %copy.182) | copy-start | bytes 3145732
  19.2 11.8 %collective-permute-start.1 = (f32[256]{0:T(256)S(1)}, f32[256]{0:T(256)S(1)}, u32[]{:S(2)}, u32[]{:S(2)}) collective-permute-start(f32[256]{0:T(256)S(1)} %add.80), channel_id=1, source_target_pairs={{0,2},{1,3},{2,0},{3,1},{4,6},{5,7},{6,4},{7,5},{8,10},{9,11},{10,... | collective-permute-start | bytes 3080 | tf_op jit(solution)/shard_map/ppermute | solution.py:16
  26.7 7.2 %collective-permute-start.5 = (bf16[16,8,256]{2,0,1:T(8,128)(2,1)S(1)}, bf16[16,8,256]{2,0,1:T(8,128)(2,1)S(1)}, u32[]{:S(2)}, u32[]{:S(2)}) collective-permute-start(bf16[16,8,256]{2,0,1:T(8,128)(2,1)S(1)} %bitcast.145), channel_id=1, source_target_pairs={{0,2},{1,3},{2,0},{3,1},{4,6},{5,7},{6,4},{7,5},{8,10},{9,11},{10,... | collective-permute-start | bytes 196616 | tf_op jit(solution)/shard_map/ppermute | solution.py:16
  31.3 5.2 %copy-start = (bf16[256,2048]{0,1:T(8,128)(2,1)}, bf16[256,2048]{0,1:T(8,128)(2,1)S(1)}, u32[]{:S(2)}) copy-start(bf16[256,2048]{0,1:T(8,128)(2,1)S(1)} %fusion.2) | copy-start | bytes 3145732
  33.9 2.6 copy-start.4
  33.9 0.7 copy-start.18
  34.6 151.9 %reduce-scatter.4.cloned.1.call-start = ((), (), s32[]{:S(2)}) async-start(), calls=%async_computation.7 | async-start | bytes 5242880 | tf_op jit(solution)/shard_map/reduce_scatter | solution.py:30
  34.7 1.8 copy-start.5
  36.5 3.6 %copy-start.1 = (bf16[256,2048]{1,0:T(8,128)(2,1)S(1)}, bf16[256,2048]{1,0:T(8,128)(2,1)}, u32[]{:S(2)}) copy-start(bf16[256,2048]{1,0:T(8,128)(2,1)} %param.5) | copy-start | bytes 3145732
  38.8 12.3 %collective-permute-start.2 = (bf16[256,8,256]{0,2,1:T(8,128)(2,1)}, bf16[256,8,256]{0,2,1:T(8,128)(2,1)}, u32[]{:S(2)}, u32[]{:S(2)}) collective-permute-start(bf16[256,8,256]{0,2,1:T(8,128)(2,1)} %get-tuple-element.30), channel_id=1, source_target_pairs={{0,1},{1,0},{2,3},{3,2},{4,5},{5,4},{6,7},{7,6},{8,9},{9,8},{10,11... | collective-permute-start | bytes 3145736 | tf_op jit(solution)/shard_map/ppermute | solution.py:16
  41.2 35.0 %collective-permute-start.3 = (bf16[256,8,256]{2,0,1:T(8,128)(2,1)}, bf16[256,8,256]{2,0,1:T(8,128)(2,1)}, u32[]{:S(2)}, u32[]{:S(2)}) collective-permute-start(bf16[256,8,256]{2,0,1:T(8,128)(2,1)} %bitcast.127), channel_id=1, source_target_pairs={{0,2},{1,3},{2,0},{3,1},{4,6},{5,7},{6,4},{7,5},{8,10},{9,11},{10,... | collective-permute-start | bytes 3145736 | tf_op jit(solution)/shard_map/ppermute | solution.py:16
  47.3 1.9 copy-start.7
  47.3 2.0 copy-start.13
  49.3 1.8 copy-start.3
  86.9 1.0 copy-start.15
  97.6 9.7 %copy-start.14 = (bf16[1,256,8,256]{3,2,1,0:T(8,128)(2,1)S(1)}, bf16[1,256,8,256]{3,2,1,0:T(8,128)(2,1)}, u32[]{:S(2)}) copy-start(bf16[1,256,8,256]{3,2,1,0:T(8,128)(2,1)} %get-tuple-element.23) | copy-start | bytes 3145732
  97.6 111.7 %reduce-scatter.6.cloned.1.call-start = ((), (), s32[]{:S(2)}) async-start(), calls=%async_computation.8 | async-start | bytes 5242880 | tf_op jit(solution)/shard_map/reduce_scatter | solution.py:30
  97.6 9.6 %copy-start.16 = (bf16[256,8,256]{0,2,1:T(8,128)(2,1)S(1)}, bf16[256,8,256]{0,2,1:T(8,128)(2,1)}, u32[]{:S(2)}) copy-start(bf16[256,8,256]{0,2,1:T(8,128)(2,1)} %copy-done.15) | copy-start | bytes 3145732
  97.7 9.6 %copy-start.17 = (f32[8,256,256]{1,2,0:T(8,128)S(1)}, f32[8,256,256]{1,2,0:T(8,128)}, u32[]{:S(2)}) copy-start(f32[8,256,256]{1,2,0:T(8,128)} %get-tuple-element.31) | copy-start | bytes 6291460
  99.5 7.8 %collective-permute-start.6 = (f32[256,8,256]{0,2,1:T(8,128)S(1)}, f32[256,8,256]{0,2,1:T(8,128)S(1)}, u32[]{:S(2)}, u32[]{:S(2)}) collective-permute-start(f32[256,8,256]{0,2,1:T(8,128)S(1)} %convolution_bitcast_fusion), channel_id=1, source_target_pairs={{0,1},{1,0},{2,3},{3,2},{4,5},{5,4},{6,7},{7,6},{8,9},{9,8},{10,11... | collective-permute-start | bytes 6291464 | tf_op jit(solution)/shard_map/ppermute | solution.py:16
  101.8 29.3 %collective-permute-start.4 = (bf16[256,8,256]{0,2,1:T(8,128)(2,1)}, bf16[256,8,256]{0,2,1:T(8,128)(2,1)}, u32[]{:S(2)}, u32[]{:S(2)}) collective-permute-start(bf16[256,8,256]{0,2,1:T(8,128)(2,1)} %get-tuple-element.8), channel_id=1, source_target_pairs={{0,2},{1,3},{2,0},{3,1},{4,6},{5,7},{6,4},{7,5},{8,10},{9,11},{10,... | collective-permute-start | bytes 3145736 | tf_op jit(solution)/shard_map/ppermute | solution.py:16
  107.3 1.4 copy-start.8
  108.7 1.0 copy-start.6
  114.6 16.5 %copy-start.2 = (bf16[256,2048]{1,0:T(8,128)(2,1)S(1)}, bf16[256,2048]{1,0:T(8,128)(2,1)}, u32[]{:S(2)}) copy-start(bf16[256,2048]{1,0:T(8,128)(2,1)} %param.5) | copy-start | bytes 3145732
  137.9 128.0 %reduce-scatter.8.cloned.1.call-start = ((), (), s32[]{:S(2)}) async-start(), calls=%async_computation.9 | async-start | bytes 2621440 | tf_op jit(solution)/shard_map/reduce_scatter | solution.py:47
  212.4 18.6 %all-to-all-start.1 = ((f32[4,4,8,8,256]{4,3,2,1,0:T(8,128)}), f32[4,4,8,8,256]{4,3,2,1,0:T(8,128)}, u32[]{:S(2)}, u32[]{:S(2)}) async-start(f32[4,4,8,8,256]{4,3,2,1,0:T(8,128)} %reduce_sum.47), calls=%async_computation.3 | async-start | bytes 2097152 | tf_op jit(solution)/shard_map/all_to_all | solution.py:49
  219.0 1.3 copy-start.10
  219.3 3.9 %collective-permute-start.7 = (f32[256]{0:T(256)S(1)}, f32[256]{0:T(256)S(1)}, u32[]{:S(2)}, u32[]{:S(2)}) collective-permute-start(f32[256]{0:T(256)S(1)} %fusion.3), channel_id=1, source_target_pairs={{0,1},{1,0},{2,3},{3,2},{4,5},{5,4},{6,7},{7,6},{8,9},{9,8},{10,11... | collective-permute-start | bytes 3080 | tf_op jit(solution)/shard_map/ppermute | solution.py:16
  223.2 51.9 %collective-permute-start.8 = (f32[256]{0:T(256)S(1)}, f32[256]{0:T(256)S(1)}, u32[]{:S(2)}, u32[]{:S(2)}) collective-permute-start(f32[256]{0:T(256)S(1)} %add.101), channel_id=1, source_target_pairs={{0,2},{1,3},{2,0},{3,1},{4,6},{5,7},{6,4},{7,5},{8,10},{9,11},{10,... | collective-permute-start | bytes 3080 | tf_op jit(solution)/shard_map/ppermute | solution.py:16
  267.9 24.3 %all-to-all-start.2 = ((f32[4,3,8,8,256]{4,3,2,1,0:T(8,128)}), f32[4,3,8,8,256]{4,3,2,1,0:T(8,128)}, u32[]{:S(2)}, u32[]{:S(2)}) async-start(f32[4,3,8,8,256]{4,3,2,1,0:T(8,128)} %maximum_bitcast_fusion), calls=%async_computation.5 | async-start | bytes 1572864 | tf_op jit(solution)/shard_map/all_to_all | solution.py:51
  272.4 2.8 copy-start.11
  277.1 2.4 copy-start.12
Sparse Core Ops, SparseCore 0:
  34.8 48.0 all-gather.1
  97.7 59.3 reduce-scatter.3
  159.8 49.3 reduce-scatter.5
  212.5 53.3 reduce-scatter.7
where the time goes:
time: 302 us; the launch traced here: 301 us
  waiting for transfers between devices  111 us (37%)
  local copies, waits for them, and re-layouts  54.8 us (18%)
  matrix products  38.8 us (13%)
  starting transfers between devices  38.2 us (13%)
  blocking collectives  30.1 us (10%)
  between operations  14.1 us (5%)
  other arithmetic  13.3 us (4%)
    ppermute x9, waiting for transfers between devices, swapped(): lax.ppermute(x, axis, [(i, i ^ 1 << stride) for i in range(lax.axis_size(...  35.1 us
    reduce_scatter x1, waiting for transfers between devices, scatter_rest(): lax.psum_scatter(a.reshape(nx, -1, rest[-1]), 'dx', scatter_dimension=0,...  33.5 us
    all_to_all x1, blocking collectives, exchange_first(): return jnp.sum(lax.all_to_all(g, 'dx', 2, 2), axis=2)  30.1 us
    ppermute x9, starting transfers between devices, swapped(): lax.ppermute(x, axis, [(i, i ^ 1 << stride) for i in range(lax.axis_size(...  29.2 us
    reduce_scatter x2, waiting for transfers between devices, scatter_first(): lax.psum_scatter(grads.reshape(ny, -1, rest[-1]), 'dy', scatter_dimension...  22.7 us
    unnamed x46, local copies, waits for them, and re-layouts  17.2 us
    all_to_all x1, waiting for transfers between devices, scatter_rest(): return jnp.sum(lax.all_to_all(g, 'dz', 0, 0), axis=0)  11.2 us
    mul x2, local copies, waits for them, and re-layouts, shards(): jnp.einsum('tbc,tbd->cbd', joined, grad_pre, preferred_element_type=jnp.f...  10.9 us
  transfers between devices with their start and end apart: 15, of which 7 were waited for; matrix products, arithmetic and copies ran while one was open for 28% of the time, Pallas kernels for 0%

commit v1 on v0

--- a/solution.py
+++ b/solution.py
@@ -57,7 +57,9 @@
     mine = lax.axis_index("dy") * lax.axis_size("dx") + lax.axis_index("dx")
     part = lax.dynamic_slice_in_dim(rows, mine * piece, piece, axis=0)
     part = swapped(part, "tensor", 1)
-    return lax.all_gather(part, ("dy", "dx"), axis=0, tiled=True)
+    return jnp.concatenate(
+        lax.all_to_all(jnp.stack([part] * lax.axis_size(("dy", "dx"))), ("dy", "dx"), 0, 0), axis=0
+    )
 
 
 def gelu_value(value):

time: 302 us -> 317 us (1.050)
  starting transfers between devices: 38.2 us -> 62.3 us
  waiting for transfers between devices: 111 us -> 92.2 us
  local copies, waits for them, and re-layouts: 54.8 us -> 60 us
  blocking collectives: 30.1 us -> 34.2 us
    ppermute x9, starting transfers between devices: 29.2 us -> 47 us  [swapped(): lax.ppermute(x, axis, [(i, i ^ 1 << stride) for i in range(lax.axis_size(...]
    reduce_scatter x2, waiting for transfers between devices: 22.7 us -> 15.9 us  [scatter_first(): lax.psum_scatter(grads.reshape(ny, -1, rest[-1]), 'dy', scatter_dimension...]
    all_gather x1 -> x0, waiting for transfers between devices: 6.66 us -> none  [partner_rows(): return lax.all_gather(part, ('dy', 'dx'), axis=0, tiled=True)]
    all_to_all x0 -> x1, starting transfers between devices: none -> 6.35 us  [partner_rows(): lax.all_to_all(jnp.stack([part] * lax.axis_size(('dy', 'dx'))), ('dy', 'd...]
    all_to_all x1, blocking collectives: 30.1 us -> 34.2 us  [exchange_first(): return jnp.sum(lax.all_to_all(g, 'dx', 2, 2), axis=2)]
    unnamed x46 -> x42, local copies, waits for them, and re-layouts: 17.2 us -> 18.3 us
  transfers between devices with their start and end apart: 15 -> 15, of which waited for: 7 -> 6; matrix products, arithmetic and copies ran while one was open for 28% -> 29% of each run, Pallas kernels for 0% -> 0%
where the time goes in v1:
time: 317 us; the launch traced here: 316 us
  waiting for transfers between devices  92.2 us (29%)
  starting transfers between devices  62.3 us (20%)
  local copies, waits for them, and re-layouts  60 us (19%)
  matrix products  39.6 us (12%)
  blocking collectives  34.2 us (11%)
  between operations  14.1 us (4%)
  other arithmetic  13.3 us (4%)
    ppermute x9, starting transfers between devices, swapped(): lax.ppermute(x, axis, [(i, i ^ 1 << stride) for i in range(lax.axis_size(...  47 us
    all_to_all x1, blocking collectives, exchange_first(): return jnp.sum(lax.all_to_all(g, 'dx', 2, 2), axis=2)  34.2 us
    ppermute x9, waiting for transfers between devices, swapped(): lax.ppermute(x, axis, [(i, i ^ 1 << stride) for i in range(lax.axis_size(...  32.4 us
    reduce_scatter x1, waiting for transfers between devices, scatter_rest(): lax.psum_scatter(a.reshape(nx, -1, rest[-1]), 'dx', scatter_dimension=0,...  31.2 us
    unnamed x42, local copies, waits for them, and re-layouts  18.3 us
    reduce_scatter x2, waiting for transfers between devices, scatter_first(): lax.psum_scatter(grads.reshape(ny, -1, rest[-1]), 'dy', scatter_dimension...  15.9 us
    all_to_all x1, waiting for transfers between devices, scatter_rest(): return jnp.sum(lax.all_to_all(g, 'dz', 0, 0), axis=0)  11.2 us
    mul x2, local copies, waits for them, and re-layouts, shards(): jnp.einsum('tbc,tbd->cbd', joined, grad_pre, preferred_element_type=jnp.f...  10.9 us
  transfers between devices with their start and end apart: 15, of which 6 were waited for; matrix products, arithmetic and copies ran while one was open for 29% of the time, Pallas kernels for 0%

profile of v1, /device:TPU:1, one launch (start us, length us, event | category | flops | bytes accessed | tf_op | source)
XLA Modules:
  0.0 315.7 jit_solution(9098644054797670777)
XLA Ops:
  7.2 1.5 copy.119
  9.0 3.3 %collective-permute-start = (f32[256]{0:T(256)S(1)}, f32[256]{0:T(256)S(1)}, u32[]{:S(2)}, u32[]{:S(2)}) collective-permute-start(f32[256]{0:T(256)S(1)} %fusion.8), channel_id=1, source_target_pairs={{0,1},{1,0},{2,3},{3,2},{4,5},{5,4},{6,7},{7,6},{8,9},{9,8},{10,11... | collective-permute-start | bytes 3080 | tf_op jit(solution)/shard_map/ppermute | solution.py:16
  12.3 5.2 %fusion.54 = (bf16[1,256,8,256]{3,2,1,0:T(8,128)(2,1)}, bf16[1,256,8,256]{3,2,1,0:T(8,128)(2,1)}, bf16[1,256,8,256]{3,2,1,0:T(8,128)(2,1)}, bf16[1,256,8,256]{3,...) fusion(bf16[3,512,8,256]{3,2,1,0:T(8,128)(2,1)} %param.4), kind=kLoop, calls=%fused_computation.80 | loop fusion | bytes 12582912 | tf_op jit(solution)/shard_map/slice | solution.py:86
  17.5 1.6 copy.186
  19.2 5.3 %collective-permute-start.1 = (f32[256]{0:T(256)S(1)}, f32[256]{0:T(256)S(1)}, u32[]{:S(2)}, u32[]{:S(2)}) collective-permute-start(f32[256]{0:T(256)S(1)} %add.80), channel_id=1, source_target_pairs={{0,2},{1,3},{2,0},{3,1},{4,6},{5,7},{6,4},{7,5},{8,10},{9,11},{10,... | collective-permute-start | bytes 3080 | tf_op jit(solution)/shard_map/ppermute | solution.py:16
  24.4 1.0 constant_dynamic-slice_fusion
  25.4 1.2 copy.136
  27.0 2.4 copy.183
  29.4 2.4 copy.182
  32.0 1.3 copy.122
  33.4 2.3 rev.8
  35.6 2.1 fusion.46
  37.7 2.3 fusion.38
  40.1 0.6 collective-permute-start.2
  40.7 1.2 stack.4
  41.8 6.3 %all-to-all-start = ((bf16[16,16,8,256]{3,1,2,0:T(8,128)(2,1)}), bf16[16,16,8,256]{3,1,2,0:T(8,128)(2,1)}, u32[]{:S(2)}, u32[]{:S(2)}) async-start(bf16[16,16,8,256]{3,1,2,0:T(8,128)(2,1)} %stack.4), calls=%async_computation | async-start | bytes 2097152 | tf_op jit(solution)/shard_map/all_to_all | solution.py:61
  48.2 1.1 copy.201
  49.3 5.6 %collective-permute-start.3 = (bf16[256,8,256]{2,0,1:T(8,128)(2,1)}, bf16[256,8,256]{2,0,1:T(8,128)(2,1)}, u32[]{:S(2)}, u32[]{:S(2)}) collective-permute-start(bf16[256,8,256]{2,0,1:T(8,128)(2,1)} %bitcast.128), channel_id=1, source_target_pairs={{0,2},{1,3},{2,0},{3,1},{4,6},{5,7},{6,4},{7,5},{8,10},{9,11},{10,... | collective-permute-start | bytes 3145736 | tf_op jit(solution)/shard_map/ppermute | solution.py:16
  54.9 2.4 copy.181
  57.3 3.1 fusion.41
  60.5 3.0 fusion.50
  63.5 1.4 all-to-all-done
  64.9 1.5 copy.138
  66.9 3.2 fusion.34
  70.0 14.3 %collective-permute-done.3 = bf16[256,8,256]{2,0,1:T(8,128)(2,1)} collective-permute-done((bf16[256,8,256]{2,0,1:T(8,128)(2,1)}, bf16[256,8,256]{2,0,1:T(8,128)(2,1)}, u32[]{:S(2)}, u32[]{:S(2)}) %collective-permute-start.3) | collective-permute-done | bytes 1048608 | tf_op jit(solution)/shard_map/ppermute | solution.py:16
  84.3 2.6 fusion.15
  87.0 1.0 copy-done.13
  87.9 4.3 %multiply_bitcast_fusion.2 = f32[512,8,256]{0,2,1:T(8,128)} fusion(bf16[256,8,256]{0,2,1:T(8,128)(2,1)S(1)} %fusion.15, bf16[256,8,256]{0,2,1:T(8,128)(2,1)} %collective-permute-done.2, bf16[256,8,256]{0,2,1:T(8,128)(2,1)} %get-tuple-element.30), kind=kOutput, calls=%fused_computation.2 | convolution fusion | flops 542113792 | bytes 7340032 | tf_op jit(solution)/shard_map/tbc,tbd->cbd/dot_general | solution.py:138
  92.2 5.4 %copy.151 = f32[512,8,256]{2,1,0:T(8,128)} copy(f32[512,8,256]{0,2,1:T(8,128)} %multiply_bitcast_fusion.2) | data formatting | bytes 8388608 | tf_op jit(solution)/shard_map/mul | solution.py:138
  97.7 1.8 convolution_bitcast_fusion
  99.6 16.5 %collective-permute-start.6 = (f32[256,8,256]{0,2,1:T(8,128)S(1)}, f32[256,8,256]{0,2,1:T(8,128)S(1)}, u32[]{:S(2)}, u32[]{:S(2)}) collective-permute-start(f32[256,8,256]{0,2,1:T(8,128)S(1)} %convolution_bitcast_fusion), channel_id=1, source_target_pairs={{0,1},{1,0},{2,3},{3,2},{4,5},{5,4},{6,7},{7,6},{8,9},{9,8},{10,11... | collective-permute-start | bytes 6291464 | tf_op jit(solution)/shard_map/ppermute | solution.py:16
  116.1 6.2 %collective-permute-start.4 = (bf16[256,8,256]{0,2,1:T(8,128)(2,1)}, bf16[256,8,256]{0,2,1:T(8,128)(2,1)}, u32[]{:S(2)}, u32[]{:S(2)}) collective-permute-start(bf16[256,8,256]{0,2,1:T(8,128)(2,1)} %get-tuple-element.8), channel_id=1, source_target_pairs={{0,2},{1,3},{2,0},{3,1},{4,6},{5,7},{6,4},{7,5},{8,10},{9,11},{10,... | collective-permute-start | bytes 3145736 | tf_op jit(solution)/shard_map/ppermute | solution.py:16
  122.3 1.4 fusion.21
  123.7 0.5 fusion.44
  124.6 1.9 copy.147
  126.5 3.6 %rev.9 = f32[256,1,2,4,256]{0,4,3,2,1:T(8,128)} reverse(f32[256,1,2,4,256]{0,4,3,2,1:T(8,128)} %copy.147), dimensions={2} | reverse | bytes 4194304 | tf_op jit(solution)/shard_map/jit(_flip)/rev | solution.py:78
  130.1 2.8 bitcast_add_fusion
  132.9 18.0 %collective-permute-done.4 = bf16[256,8,256]{0,2,1:T(8,128)(2,1)} collective-permute-done((bf16[256,8,256]{0,2,1:T(8,128)(2,1)}, bf16[256,8,256]{0,2,1:T(8,128)(2,1)}, u32[]{:S(2)}, u32[]{:S(2)}) %collective-permute-start.4) | collective-permute-done | bytes 1048608 | tf_op jit(solution)/shard_map/ppermute | solution.py:16
  151.0 2.3 multiply_bitcast_fusion.1
  153.2 4.4 %copy.153 = f32[512,8,256]{2,1,0:T(8,128)} copy(f32[512,8,256]{2,0,1:T(8,128)S(1)} %multiply_bitcast_fusion.1) | data formatting | bytes 8388608 | tf_op jit(solution)/shard_map/mul | solution.py:161
  157.7 2.3 copy.156
  160.0 4.5 %multiply_bitcast_fusion = f32[512,8,256]{0,2,1:T(8,128)} fusion(bf16[256,8,256]{0,2,1:T(8,128)(2,1)} %copy-done.4, bf16[256,8,256]{2,0,1:T(8,128)(2,1)} %bitcast.139, bf16[256,8,256]{2,0,1:T(8,128)(2,1)} %copy.156), kind=kOutput, calls=%fused_computation | convolution fusion | flops 542113792 | bytes 7340032 | tf_op jit(solution)/shard_map/tbc,tbd->cbd/dot_general | solution.py:138
  164.5 5.5 %copy.157 = f32[512,8,256]{2,1,0:T(8,128)} copy(f32[512,8,256]{0,2,1:T(8,128)} %multiply_bitcast_fusion) | data formatting | bytes 8388608 | tf_op jit(solution)/shard_map/mul | solution.py:138
  170.0 2.5 copy.158
  172.5 34.2 %all_to_all.20 = f32[4,4,4,8,8,256]{5,4,3,1,0,2:T(8,128)} all-to-all(f32[4,4,4,8,8,256]{5,4,3,1,0,2:T(8,128)S(1)} %copy.158), channel_id=1, replica_groups=mesh['dy'=4,'dz'=4,'dx'=4,'tensor'=4] {'dx'}, dimensions={2} | all-to-all | bytes 8388608 | tf_op jit(solution)/shard_map/all_to_all | solution.py:39
  206.7 3.6 %reduce_sum.47 = f32[4,4,8,8,256]{4,3,2,1,0:T(8,128)} reduce(f32[4,4,4,8,8,256]{5,4,3,1,0,2:T(8,128)} %all_to_all.20, f32[]{:T(128)} %constant.7.clone.1), dimensions={2}, to_apply=%region_4.5 | reduce | flops 786432 | bytes 5242884 | tf_op jit(solution)/shard_map/reduce_sum | solution.py:39
  210.3 15.9 %reduce-scatter.6.cloned.1.call-done = f32[1,1024,256]{2,1,0:T(8,128)} async-done(((f32[4,1024,256]{2,1,0:T(8,128)}), f32[1,1024,256]{2,1,0:T(8,128)}) %reduce-scatter.6.cloned.1.call-update) | async-done | bytes 1048592 | tf_op jit(solution)/shard_map/reduce_scatter | solution.py:30
  226.2 1.7 pad_maximum_fusion
  227.9 1.4 copy.180
  229.3 4.3 %all-to-all-start.2 = ((f32[4,4,8,8,256]{4,3,2,1,0:T(8,128)}), f32[4,4,8,8,256]{4,3,2,1,0:T(8,128)}, u32[]{:S(2)}, u32[]{:S(2)}) async-start(f32[4,4,8,8,256]{4,3,2,1,0:T(8,128)} %reduce_sum.47), calls=%async_computation.4 | async-start | bytes 2097152 | tf_op jit(solution)/shard_map/all_to_all | solution.py:49
  233.6 2.3 copy.149
  236.2 3.7 %collective-permute-start.7 = (f32[256]{0:T(256)S(1)}, f32[256]{0:T(256)S(1)}, u32[]{:S(2)}, u32[]{:S(2)}) collective-permute-start(f32[256]{0:T(256)S(1)} %fusion.3), channel_id=1, source_target_pairs={{0,1},{1,0},{2,3},{3,2},{4,5},{5,4},{6,7},{7,6},{8,9},{9,8},{10,11... | collective-permute-start | bytes 3080 | tf_op jit(solution)/shard_map/ppermute | solution.py:16
  240.0 3.0 fusion.39
  243.0 5.5 %collective-permute-start.8 = (f32[256]{0:T(256)S(1)}, f32[256]{0:T(256)S(1)}, u32[]{:S(2)}, u32[]{:S(2)}) collective-permute-start(f32[256]{0:T(256)S(1)} %add.101), channel_id=1, source_target_pairs={{0,2},{1,3},{2,0},{3,1},{4,6},{5,7},{6,4},{7,5},{8,10},{9,11},{10,... | collective-permute-start | bytes 3080 | tf_op jit(solution)/shard_map/ppermute | solution.py:16
  248.5 1.3 reduce_sum.48
  249.8 31.2 %reduce-scatter.8.cloned.1.call-done = f32[1,512,256]{2,1,0:T(8,128)} async-done(((f32[4,512,256]{2,1,0:T(8,128)}), f32[1,512,256]{2,1,0:T(8,128)}) %reduce-scatter.8.cloned.1.call-update) | async-done | bytes 524304 | tf_op jit(solution)/shard_map/reduce_scatter | solution.py:47
  281.0 2.0 maximum_bitcast_fusion
  283.0 4.5 %all-to-all-start.3 = ((f32[4,3,8,8,256]{4,3,2,1,0:T(8,128)}), f32[4,3,8,8,256]{4,3,2,1,0:T(8,128)}, u32[]{:S(2)}, u32[]{:S(2)}) async-start(f32[4,3,8,8,256]{4,3,2,1,0:T(8,128)} %maximum_bitcast_fusion), calls=%async_computation.6 | async-start | bytes 1572864 | tf_op jit(solution)/shard_map/all_to_all | solution.py:51
  287.5 2.8 convolution_add_fusion
  290.3 1.9 fusion.7
  292.2 2.4 copy.161
  294.6 1.4 copy.162
  296.0 11.2 %all-to-all-done.3 = f32[4,3,8,8,256]{4,3,2,1,0:T(8,128)} async-done(((f32[4,3,8,8,256]{4,3,2,1,0:T(8,128)}), f32[4,3,8,8,256]{4,3,2,1,0:T(8,128)}, u32[]{:S(2)}, u32[]{:S(2)}) %all-to-all-start.3) | async-done | bytes 786464 | tf_op jit(solution)/shard_map/all_to_all | solution.py:51
  307.2 1.9 reduce_sum.49
  (57 shorter events, 2.3 us)
Async XLA Ops:
  9.0 10.2 %collective-permute-start = (f32[256]{0:T(256)S(1)}, f32[256]{0:T(256)S(1)}, u32[]{:S(2)}, u32[]{:S(2)}) collective-permute-start(f32[256]{0:T(256)S(1)} %fusion.8), channel_id=1, source_target_pairs={{0,1},{1,0},{2,3},{3,2},{4,5},{5,4},{6,7},{7,6},{8,9},{9,8},{10,11... | collective-permute-start | bytes 3080 | tf_op jit(solution)/shard_map/ppermute | solution.py:16
  19.1 12.7 %copy-start.7 = (bf16[1,256,8,256]{1,3,2,0:T(8,128)(2,1)}, bf16[1,256,8,256]{1,3,2,0:T(8,128)(2,1)S(1)}, u32[]{:S(2)}) copy-start(bf16[1,256,8,256]{1,3,2,0:T(8,128)(2,1)S(1)} %copy.186) | copy-start | bytes 3145732
  19.2 12.7 %collective-permute-start.1 = (f32[256]{0:T(256)S(1)}, f32[256]{0:T(256)S(1)}, u32[]{:S(2)}, u32[]{:S(2)}) collective-permute-start(f32[256]{0:T(256)S(1)} %add.80), channel_id=1, source_target_pairs={{0,2},{1,3},{2,0},{3,1},{4,6},{5,7},{6,4},{7,5},{8,10},{9,11},{10,... | collective-permute-start | bytes 3080 | tf_op jit(solution)/shard_map/ppermute | solution.py:16
  26.7 14.0 %collective-permute-start.5 = (bf16[16,8,256]{2,1,0:T(8,128)(2,1)S(1)}, bf16[16,8,256]{2,1,0:T(8,128)(2,1)S(1)}, u32[]{:S(2)}, u32[]{:S(2)}) collective-permute-start(bf16[16,8,256]{2,1,0:T(8,128)(2,1)S(1)} %bitcast.147), channel_id=1, source_target_pairs={{0,2},{1,3},{2,0},{3,1},{4,6},{5,7},{6,4},{7,5},{8,10},{9,11},{10,... | collective-permute-start | bytes 196616 | tf_op jit(solution)/shard_map/ppermute | solution.py:16
  32.0 5.7 %copy-start = (bf16[256,2048]{0,1:T(8,128)(2,1)}, bf16[256,2048]{0,1:T(8,128)(2,1)S(1)}, u32[]{:S(2)}) copy-start(bf16[256,2048]{0,1:T(8,128)(2,1)S(1)} %fusion.2) | copy-start | bytes 3145732
  35.6 2.1 copy-start.3
  40.0 8.2 %copy-start.1 = (bf16[256,2048]{1,0:T(8,128)(2,1)S(1)}, bf16[256,2048]{1,0:T(8,128)(2,1)}, u32[]{:S(2)}) copy-start(bf16[256,2048]{1,0:T(8,128)(2,1)} %param.5) | copy-start | bytes 3145732
  40.1 26.4 %collective-permute-start.2 = (bf16[256,8,256]{0,2,1:T(8,128)(2,1)}, bf16[256,8,256]{0,2,1:T(8,128)(2,1)}, u32[]{:S(2)}, u32[]{:S(2)}) collective-permute-start(bf16[256,8,256]{0,2,1:T(8,128)(2,1)} %get-tuple-element.30), channel_id=1, source_target_pairs={{0,1},{1,0},{2,3},{3,2},{4,5},{5,4},{6,7},{7,6},{8,9},{9,8},{10,11... | collective-permute-start | bytes 3145736 | tf_op jit(solution)/shard_map/ppermute | solution.py:16
  41.8 23.1 %all-to-all-start = ((bf16[16,16,8,256]{3,1,2,0:T(8,128)(2,1)}), bf16[16,16,8,256]{3,1,2,0:T(8,128)(2,1)}, u32[]{:S(2)}, u32[]{:S(2)}) async-start(bf16[16,16,8,256]{3,1,2,0:T(8,128)(2,1)} %stack.4), calls=%async_computation | async-start | bytes 2097152 | tf_op jit(solution)/shard_map/all_to_all | solution.py:61
  48.2 162.1 %reduce-scatter.4.cloned.1.call-start = ((), (), s32[]{:S(2)}) async-start(), calls=%async_computation.7 | async-start | bytes 5242880 | tf_op jit(solution)/shard_map/reduce_scatter | solution.py:30
  49.3 35.0 %collective-permute-start.3 = (bf16[256,8,256]{2,0,1:T(8,128)(2,1)}, bf16[256,8,256]{2,0,1:T(8,128)(2,1)}, u32[]{:S(2)}, u32[]{:S(2)}) collective-permute-start(bf16[256,8,256]{2,0,1:T(8,128)(2,1)} %bitcast.128), channel_id=1, source_target_pairs={{0,2},{1,3},{2,0},{3,1},{4,6},{5,7},{6,4},{7,5},{8,10},{9,11},{10,... | collective-permute-start | bytes 3145736 | tf_op jit(solution)/shard_map/ppermute | solution.py:16
  57.3 3.1 copy-start.11
  64.9 1.9 copy-start.6
  66.9 17.5 %copy-start.16 = (f32[8,256,256]{2,1,0:T(8,128)S(1)}, f32[8,256,256]{2,1,0:T(8,128)}, u32[]{:S(2)}) copy-start(f32[8,256,256]{2,1,0:T(8,128)} %fusion.41) | copy-start | bytes 6291460
  86.9 1.0 copy-start.13
  97.7 24.6 %copy-start.12 = (bf16[1,256,8,256]{3,2,1,0:T(8,128)(2,1)S(1)}, bf16[1,256,8,256]{3,2,1,0:T(8,128)(2,1)}, u32[]{:S(2)}) copy-start(bf16[1,256,8,256]{3,2,1,0:T(8,128)(2,1)} %get-tuple-element.23) | copy-start | bytes 3145732
  97.7 128.5 %reduce-scatter.6.cloned.1.call-start = ((), (), s32[]{:S(2)}) async-start(), calls=%async_computation.8 | async-start | bytes 5242880 | tf_op jit(solution)/shard_map/reduce_scatter | solution.py:30
  97.7 24.5 %copy-start.14 = (bf16[256,8,256]{0,2,1:T(8,128)(2,1)S(1)}, bf16[256,8,256]{0,2,1:T(8,128)(2,1)}, u32[]{:S(2)}) copy-start(bf16[256,8,256]{0,2,1:T(8,128)(2,1)} %copy-done.13) | copy-start | bytes 3145732
  97.7 24.5 %copy-start.15 = (f32[8,256,256]{1,2,0:T(8,128)S(1)}, f32[8,256,256]{1,2,0:T(8,128)}, u32[]{:S(2)}) copy-start(f32[8,256,256]{1,2,0:T(8,128)} %get-tuple-element.31) | copy-start | bytes 6291460
  99.6 22.7 %collective-permute-start.6 = (f32[256,8,256]{0,2,1:T(8,128)S(1)}, f32[256,8,256]{0,2,1:T(8,128)S(1)}, u32[]{:S(2)}, u32[]{:S(2)}) collective-permute-start(f32[256,8,256]{0,2,1:T(8,128)S(1)} %convolution_bitcast_fusion), channel_id=1, source_target_pairs={{0,1},{1,0},{2,3},{3,2},{4,5},{5,4},{6,7},{7,6},{8,9},{9,8},{10,11... | collective-permute-start | bytes 6291464 | tf_op jit(solution)/shard_map/ppermute | solution.py:16
  116.1 34.9 %collective-permute-start.4 = (bf16[256,8,256]{0,2,1:T(8,128)(2,1)}, bf16[256,8,256]{0,2,1:T(8,128)(2,1)}, u32[]{:S(2)}, u32[]{:S(2)}) collective-permute-start(bf16[256,8,256]{0,2,1:T(8,128)(2,1)} %get-tuple-element.8), channel_id=1, source_target_pairs={{0,2},{1,3},{2,0},{3,1},{4,6},{5,7},{6,4},{7,5},{8,10},{9,11},{10,... | collective-permute-start | bytes 3145736 | tf_op jit(solution)/shard_map/ppermute | solution.py:16
  122.3 1.4 copy-start.5
  123.7 1.0 copy-start.4
  130.1 20.9 %copy-start.2 = (bf16[256,2048]{1,0:T(8,128)(2,1)S(1)}, bf16[256,2048]{1,0:T(8,128)(2,1)}, u32[]{:S(2)}) copy-start(bf16[256,2048]{1,0:T(8,128)(2,1)} %param.5) | copy-start | bytes 3145732
  157.7 123.3 %reduce-scatter.8.cloned.1.call-start = ((), (), s32[]{:S(2)}) async-start(), calls=%async_computation.9 | async-start | bytes 2621440 | tf_op jit(solution)/shard_map/reduce_scatter | solution.py:47
  229.3 19.1 %all-to-all-start.2 = ((f32[4,4,8,8,256]{4,3,2,1,0:T(8,128)}), f32[4,4,8,8,256]{4,3,2,1,0:T(8,128)}, u32[]{:S(2)}, u32[]{:S(2)}) async-start(f32[4,4,8,8,256]{4,3,2,1,0:T(8,128)} %reduce_sum.47), calls=%async_computation.4 | async-start | bytes 2097152 | tf_op jit(solution)/shard_map/all_to_all | solution.py:49
  235.9 4.1 %copy-start.8 = (bf16[1,256,8,256]{1,3,2,0:T(8,128)(2,1)S(1)}, bf16[1,256,8,256]{1,3,2,0:T(8,128)(2,1)}, u32[]{:S(2)}) copy-start(bf16[1,256,8,256]{1,3,2,0:T(8,128)(2,1)} %copy-done.7) | copy-start | bytes 3145732
  236.2 6.7 %collective-permute-start.7 = (f32[256]{0:T(256)S(1)}, f32[256]{0:T(256)S(1)}, u32[]{:S(2)}, u32[]{:S(2)}) collective-permute-start(f32[256]{0:T(256)S(1)} %fusion.3), channel_id=1, source_target_pairs={{0,1},{1,0},{2,3},{3,2},{4,5},{5,4},{6,7},{7,6},{8,9},{9,8},{10,11... | collective-permute-start | bytes 3080 | tf_op jit(solution)/shard_map/ppermute | solution.py:16
  243.0 47.3 %collective-permute-start.8 = (f32[256]{0:T(256)S(1)}, f32[256]{0:T(256)S(1)}, u32[]{:S(2)}, u32[]{:S(2)}) collective-permute-start(f32[256]{0:T(256)S(1)} %add.101), channel_id=1, source_target_pairs={{0,2},{1,3},{2,0},{3,1},{4,6},{5,7},{6,4},{7,5},{8,10},{9,11},{10,... | collective-permute-start | bytes 3080 | tf_op jit(solution)/shard_map/ppermute | solution.py:16
  283.0 24.3 %all-to-all-start.3 = ((f32[4,3,8,8,256]{4,3,2,1,0:T(8,128)}), f32[4,3,8,8,256]{4,3,2,1,0:T(8,128)}, u32[]{:S(2)}, u32[]{:S(2)}) async-start(f32[4,3,8,8,256]{4,3,2,1,0:T(8,128)} %maximum_bitcast_fusion), calls=%async_computation.6 | async-start | bytes 1572864 | tf_op jit(solution)/shard_map/all_to_all | solution.py:51
  287.5 2.8 copy-start.9
  292.2 2.4 copy-start.10
Sparse Core Ops, SparseCore 0:
  97.8 67.1 reduce-scatter.3
  167.7 58.4 reduce-scatter.5
  229.5 51.4 reduce-scatter.7
